TPU v7x, 512 devices: a whole 4x8x8 slice. The times are simulated.
512 devices in a mesh: member: 16 (over x_lo, y), dp: 32 (over z, x_hi, core).
Axes of the slice: x: 4 (x_hi: 2, x_lo: 2; x = x_hi * 2 + x_lo), y: 8, z: 8, core: 2. Of those that a mesh axis runs over, the one named last changes fastest.
Arguments:
- inputs: bfloat16 [8192, 64], P('dp'), may hold values from -6 to 6
- observed: float32 [64, 8192], P('member', 'dp'), may hold values from -6 to 6
- noise: bfloat16 [2, 32, 64, 8192], P(None, None, 'member', 'dp'), may hold values from -4 to 4
- w_in: float32 [32, 64, 4096], P('member', None, 'dp'), may hold values from -0.75 to 0.75
- b_in: float32 [32, 4096], P('member', 'dp'), may hold values from -3 to 3
- w_out: float32 [32, 64, 4096], P('member', None, 'dp'), may hold values from -0.09375 to 0.09375
- b_out: float32 [32, 64], P('member'), may hold values from -3 to 3
Outputs:
- new_w_in: float32 [32, 64, 4096], P('member', None, 'dp')
- new_b_in: float32 [32, 4096], P('member', 'dp')
- new_w_out: float32 [32, 64, 4096], P('member', None, 'dp')
- new_b_out: float32 [32, 64], P('member')
All inputs are finite; a program needn't handle non-finite values.
Results may differ from a plain program's by a relative error of at most 0.00056.
Values may be sent and summed in bfloat16 or wider, within the bound.
No kernel may reach another device: no remote copies, remote signals or barrier semaphores. Data moves between devices by JAX's collectives and lax.ppermute only.
A program may use at most 64 MiB of HBM per device.

v0:
```python
import jax
import jax.numpy as jnp
from jax import lax
from jax.sharding import PartitionSpec as P

UPDATES = 2
ridge_level = 0.5


def solve_gain(gram, cross):
    eye = jnp.eye(gram.shape[0], dtype=gram.dtype)
    factor = jnp.linalg.cholesky(gram + ridge_level * eye)
    middle = lax.linalg.triangular_solve(factor, cross, left_side=True, lower=True)
    return lax.linalg.triangular_solve(factor, middle, left_side=True, lower=True, transpose_a=True)


def pack(w_in, b_in, w_out, b_out):
    n = w_in.shape[0]
    return jnp.concatenate(
        [w_in.reshape(n, -1), w_out.reshape(n, -1), b_in.reshape(n, -1), b_out.reshape(n, -1)],
        axis=1,
    )


def unpack(flat, f_in, hid, outs):
    n = flat.shape[0]
    a = f_in * hid
    b = a + outs * hid
    c = b + hid
    return (
        flat[:, :a].reshape(n, f_in, hid),
        flat[:, b:c].reshape(n, hid),
        flat[:, a:b].reshape(n, outs, hid),
        flat[:, c:].reshape(n, outs),
    )


def predict(inputs, own_flat, b_out, f_in, hid, outs):
    n = own_flat.shape[0]
    a = f_in * hid
    b = a + outs * hid
    rounded = own_flat[:, : b + hid].astype(jnp.bfloat16)
    gathered = lax.all_gather(rounded, "dp", axis=0, tiled=False)
    d = gathered.shape[0]
    w_in = gathered[:, :, :a].reshape(d, n, f_in, hid)
    w_out = gathered[:, :, a:b].reshape(d, n, outs, hid)
    b_in = gathered[:, :, b : b + hid]
    pre = jnp.einsum("sf,dnfh->nsdh", inputs, w_in, preferred_element_type=jnp.float32)
    pre = pre + jnp.transpose(b_in, (1, 0, 2)).astype(jnp.float32)[:, None, :, :]
    hidden = jnp.tanh(pre).astype(jnp.bfloat16)
    pred = jnp.einsum("dnoh,nsdh->nos", w_out, hidden, preferred_element_type=jnp.float32)
    return pred + b_out[:, :, None]


def on_device(inputs, observed, noise, w_in, b_in, w_out, b_out):
    per_device = w_in.shape[0]
    f_in, hid = (w_in.shape[1], w_in.shape[2])
    outs = w_out.shape[1]
    count = observed.shape[0] * lax.axis_size("member") * observed.shape[1] * lax.axis_size("dp")
    first = lax.axis_index("member") * per_device
    own = pack(w_in, b_in, w_out, b_out)
    whole = lax.all_gather(own, "member", axis=0, tiled=True)
    for update in range(UPDATES):
        own_b_out = own[:, -outs:]
        predicted = predict(inputs, own, own_b_out, f_in, hid, outs)
        collected = lax.all_to_all(predicted, "member", split_axis=1, concat_axis=0, tiled=True)
        mean_pred = jnp.mean(collected, axis=0)
        anomaly = (collected - mean_pred[None]).reshape(collected.shape[0], -1)
        misfit = (observed[None] + noise[update].astype(jnp.float32) - collected).reshape(
            collected.shape[0], -1
        )
        gram_part = lax.dot_general(
            anomaly, anomaly, (((1,), (1,)), ((), ())), precision=lax.Precision.HIGHEST
        )
        cross_part = lax.dot_general(
            anomaly, misfit, (((1,), (1,)), ((), ())), precision=lax.Precision.HIGHEST
        )
        gram, cross = lax.psum((gram_part, cross_part), ("member", "dp"))
        gain = solve_gain(gram / count, cross / count)
        if update + 1 < UPDATES:
            moved = lax.dot_general(
                gain, whole, (((0,), (0,)), ((), ())), precision=lax.Precision.HIGHEST
            )
            whole = whole + moved
            own = lax.dynamic_slice_in_dim(whole, first, per_device, 0)
        else:
            columns = lax.dynamic_slice_in_dim(gain, first, per_device, 1)
            moved = lax.dot_general(
                columns, whole, (((0,), (0,)), ((), ())), precision=lax.Precision.HIGHEST
            )
            own = own + moved
    return unpack(own, f_in, hid, outs)


def solution(mesh):
    placed = (
        P("dp", None),
        P("member", "dp"),
        P(None, None, "member", "dp"),
        P("member", None, "dp"),
        P("member", "dp"),
        P("member", None, "dp"),
        P("member", None),
    )
    return jax.shard_map(
        on_device,
        mesh=mesh,
        in_specs=placed,
        out_specs=(
            P("member", None, "dp"),
            P("member", "dp"),
            P("member", None, "dp"),
            P("member", None),
        ),
        check_vma=False,
    )
```

profile of v0, /device:TPU:1, one launch (start us, length us, event | category | flops | bytes accessed | tf_op | source)
XLA Modules:
  0.0 511.3 jit_solution(14198276268625181387)
XLA Ops:
  7.2 0.7 convert_bitcast_fusion.2
  7.9 0.8 convert.20
  8.8 0.8 convert.19
  10.4 1.0 copy_bitcast_fusion.2
  11.4 1.4 maximum_bitcast_fusion
  12.8 90.6 %all-gather.7.cloned.1.call-done = bf16[32,2,16512]{2,1,0:T(2,128)(2,1)} async-done(((bf16[1,2,16512]{2,1,0:T(2,128)(2,1)}), bf16[32,2,16512]{2,1,0:T(2,128)(2,1)}) %all-gather.7.cloned.1.call-update) | async-done | bytes 2113552 | tf_op jit(solution)/shard_map/all_gather | solution.py:43
  103.4 0.7 convert_bitcast_fusion.1
  104.1 2.9 fusion.60
  107.1 0.8 reshape.148
  107.9 0.8 reshape.147
  108.8 2.5 fusion.20
  111.3 0.7 copy.43
  112.1 6.6 %all-to-all-start = ((f32[2,64,256]{2,0,1:T(2,128)}), f32[2,64,256]{2,0,1:T(2,128)S(1)}, u32[]{:S(2)}, u32[]{:S(2)}) async-start(f32[2,64,256]{2,0,1:T(2,128)} %copy.43), calls=%async_computation | async-start | bytes 262144 | tf_op jit(solution)/shard_map/all_to_all | solution.py:66
  118.8 47.6 %all-gather.9.cloned.1.call-done = f32[16,2,16576]{2,1,0:T(2,128)} async-done(((f32[1,2,16576]{2,1,0:T(2,128)}), f32[16,2,16576]{2,1,0:T(2,128)}) %all-gather.9.cloned.1.call-update) | async-done | bytes 2121744 | tf_op jit(solution)/shard_map/all_gather | solution.py:62
  166.4 3.7 reshape.128
  170.7 107.1 %all-reduce.1 = (f32[32,32]{0,1:T(8,128)S(1)}, f32[32,32]{0,1:T(8,128)S(1)}) all-reduce(f32[32,32]{0,1:T(8,128)S(1)} %convolution_bitcast_fusion.3, f32[32,32]{0,1:T(8,128)S(1)} %convolution_bitcast_fusion.2), channel_id=1, replica_groups=mesh['member'=16,'dp'=32] {'member','dp'}, use_global_device_ids=true, to_apply=%region_1.0 | all-reduce | flops 2048 | bytes 16384 | tf_op jit(solution)/shard_map/psum | solution.py:78
  277.9 2.9 cholesky.44
  282.1 2.4 custom-call.11
  285.0 4.2 convolution_add_fusion
  289.1 0.7 fusion.35
  289.9 80.4 %all-gather.11.cloned.1.call-done = bf16[32,2,16512]{2,1,0:T(2,128)(2,1)} async-done(((bf16[1,2,16512]{2,1,0:T(2,128)(2,1)}), bf16[32,2,16512]{2,1,0:T(2,128)(2,1)}) %all-gather.11.cloned.1.call-update) | async-done | bytes 2113552 | tf_op jit(solution)/shard_map/all_gather | solution.py:43
  370.3 4.0 fusion.59
  374.4 2.6 reshape.116
  377.0 0.7 convert_bitcast_fusion
  377.8 1.6 reshape.149
  379.4 3.2 fusion.1
  382.6 0.8 fusion.17
  383.6 13.8 %all_to_all.30 = f32[2,64,256]{2,0,1:T(2,128)S(1)} all-to-all(f32[2,64,256]{2,0,1:T(2,128)S(1)} %copy.55), channel_id=1, replica_groups=mesh['member'=16,'dp'=32] {'member'}, dimensions={1} | all-to-all | bytes 262144 | tf_op jit(solution)/shard_map/all_to_all | solution.py:66
  398.0 96.0 %all-reduce = (f32[32,32]{0,1:T(8,128)S(1)}, f32[32,32]{0,1:T(8,128)S(1)}) all-reduce(f32[32,32]{0,1:T(8,128)S(1)} %convolution_bitcast_fusion.1, f32[32,32]{0,1:T(8,128)S(1)} %convolution_bitcast_fusion), channel_id=1, replica_groups=mesh['member'=16,'dp'=32] {'member','dp'}, use_global_device_ids=true, to_apply=%region_6.10 | all-reduce | flops 2048 | bytes 16384 | tf_op jit(solution)/shard_map/psum | solution.py:78
  494.1 2.9 cholesky.55
  498.4 2.4 custom-call.13
  501.3 1.1 convolution_add_fusion.1
  (56 shorter events, 8.5 us)
Async XLA Ops:
  7.2 101.6 %copy-start = (bf16[256,64]{0,1:T(8,128)(2,1)S(1)}, bf16[256,64]{0,1:T(8,128)(2,1)}, u32[]{:S(2)}) copy-start(bf16[256,64]{0,1:T(8,128)(2,1)} %param.12) | copy-start | bytes 98308
  7.2 96.2 %all-gather.7.cloned.1.call-start = ((), (), s32[]{:S(2)}) async-start(), calls=%async_computation.2 | async-start | bytes 2179584 | tf_op jit(solution)/shard_map/all_gather | solution.py:43
  10.3 156.0 %all-gather.9.cloned.1.call-start = ((), (), s32[]{:S(2)}) async-start(), calls=%async_computation.3 | async-start | bytes 2263040 | tf_op jit(solution)/shard_map/all_gather | solution.py:62
  107.1 1.7 copy-start.4
  108.8 9.9 %copy-start.2 = (bf16[2,32,4,256]{3,2,1,0:T(4,128)(2,1)S(1)}, bf16[2,32,4,256]{3,2,1,0:T(4,128)(2,1)}, u32[]{:S(2)}) copy-start(bf16[2,32,4,256]{3,2,1,0:T(4,128)(2,1)} %param.14) | copy-start | bytes 393220
  112.1 58.0 %all-to-all-start = ((f32[2,64,256]{2,0,1:T(2,128)}), f32[2,64,256]{2,0,1:T(2,128)S(1)}, u32[]{:S(2)}, u32[]{:S(2)}) async-start(f32[2,64,256]{2,0,1:T(2,128)} %copy.43), calls=%async_computation | async-start | bytes 262144 | tf_op jit(solution)/shard_map/all_to_all | solution.py:66
  118.6 251.7 %all-gather.11.cloned.1.call-start = ((), (), s32[]{:S(2)}) async-start(), calls=%async_computation.4 | async-start | bytes 2179584 | tf_op jit(solution)/shard_map/all_gather | solution.py:43
  118.7 51.4 %copy-start.3 = (f32[4,256]{1,0:T(4,128)S(1)}, f32[4,256]{1,0:T(4,128)}, u32[]{:S(2)}) copy-start(f32[4,256]{1,0:T(4,128)} %param.13) | copy-start | bytes 12292
  379.4 3.2 copy-start.1
Sparse Core Ops, SparseCore 0:
  11.4 91.9 all-gather.6
  105.5 60.8 all-gather.8
  290.0 80.3 all-gather.10
where the time goes:
time: 512 us; the launch traced here: 511 us
  waiting for transfers between devices  219 us (43%)
  blocking collectives  217 us (42%)
  local copies, waits for them, and re-layouts  21.8 us (4%)
  other arithmetic  19.5 us (4%)
  between operations  14 us (3%)
  matrix products  13.7 us (3%)
  starting transfers between devices  6.69 us (1%)
    psum x2, blocking collectives, on_device(): gram, cross = lax.psum((gram_part, cross_part), ('member', 'dp'))  203 us
    all_gather x2, waiting for transfers between devices, predict(): gathered = lax.all_gather(rounded, 'dp', axis=0, tiled=False)  171 us
    all_gather x1, waiting for transfers between devices, on_device(): whole = lax.all_gather(own, 'member', axis=0, tiled=True)  47.6 us
    all_to_all x1, blocking collectives, on_device(): lax.all_to_all(predicted, 'member', split_axis=1, concat_axis=0, tiled=True)  13.8 us
  transfers between devices with their start and end apart: 4, of which 3 were waited for; matrix products, arithmetic and copies ran while one was open for 3% of the time, Pallas kernels for 0%

commit v1 on v0

--- a/solution.py
+++ b/solution.py
@@ -5,6 +5,10 @@
 
 UPDATES = 2
 ridge_level = 0.5
+frames_close = lambda x_part, row_dim: jnp.concatenate(
+    lax.all_to_all(jnp.stack([x_part for _ in range(lax.axis_size("member"))]), "member", 0, 0),
+    axis=row_dim,
+)
 
 
 def solve_gain(gram, cross):
@@ -59,7 +63,7 @@
     count = observed.shape[0] * lax.axis_size("member") * observed.shape[1] * lax.axis_size("dp")
     first = lax.axis_index("member") * per_device
     own = pack(w_in, b_in, w_out, b_out)
-    whole = lax.all_gather(own, "member", axis=0, tiled=True)
+    whole = frames_close(own, row_dim=0)
     for update in range(UPDATES):
         own_b_out = own[:, -outs:]
         predicted = predict(inputs, own, own_b_out, f_in, hid, outs)

time: 512 us -> 466 us (0.910)
  waiting for transfers between devices: 219 us -> 170 us
  blocking collectives: 217 us -> 206 us
  starting transfers between devices: 6.69 us -> 14.2 us
    all_gather x1 -> x0, waiting for transfers between devices: 47.6 us -> none  [on_device(): whole = lax.all_gather(own, 'member', axis=0, tiled=True)]
    psum x2, blocking collectives: 203 us -> 192 us  [on_device(): gram, cross = lax.psum((gram_part, cross_part), ('member', 'dp'))]
    all_to_all x0 -> x1, starting transfers between devices: none -> 8.68 us  [lax.all_to_all(jnp.stack([x_part for _ in range(lax.axis_size('member'))]...]
    all_gather x2, waiting for transfers between devices: 171 us -> 165 us  [predict(): gathered = lax.all_gather(rounded, 'dp', axis=0, tiled=False)]
  transfers between devices with their start and end apart: 4 -> 4, of which waited for: 3 -> 3; matrix products, arithmetic and copies ran while one was open for 3% -> 4% of each run, Pallas kernels for 0% -> 0%
where the time goes in v1:
time: 466 us; the launch traced here: 465 us
  blocking collectives  206 us (44%)
  waiting for transfers between devices  170 us (36%)
  local copies, waits for them, and re-layouts  26.3 us (6%)
  other arithmetic  18.9 us (4%)
  matrix products  15.3 us (3%)
  between operations  14.3 us (3%)
  starting transfers between devices  14.2 us (3%)
    psum x2, blocking collectives, on_device(): gram, cross = lax.psum((gram_part, cross_part), ('member', 'dp'))  192 us
    all_gather x2, waiting for transfers between devices, predict(): gathered = lax.all_gather(rounded, 'dp', axis=0, tiled=False)  165 us
    all_to_all x1, blocking collectives, on_device(): lax.all_to_all(predicted, 'member', split_axis=1, concat_axis=0, tiled=True)  13.8 us
  transfers between devices with their start and end apart: 4, of which 3 were waited for; matrix products, arithmetic and copies ran while one was open for 4% of the time, Pallas kernels for 0%

profile of v1, /device:TPU:1, one launch (start us, length us, event | category | flops | bytes accessed | tf_op | source)
XLA Modules:
  0.0 465.0 jit_solution(12937209590407473196)
XLA Ops:
  7.9 0.8 convert.20
  8.8 0.8 convert.19
  10.3 1.0 copy_bitcast_fusion.2
  11.3 0.8 pad_maximum_fusion
  12.1 1.9 stack.2
  14.0 8.7 %all-to-all-start = ((f32[16,2,16576]{2,1,0:T(2,128)}), f32[16,2,16576]{2,1,0:T(2,128)S(1)}, u32[]{:S(2)}, u32[]{:S(2)}) async-start(f32[16,2,16576]{2,1,0:T(2,128)} %stack.2), calls=%async_computation | async-start | bytes 4259840 | tf_op jit(solution)/shard_map/all_to_all | solution.py:9
  22.7 84.6 %all-gather.5.cloned.1.call-done = bf16[32,2,16512]{2,1,0:T(2,128)(2,1)} async-done(((bf16[1,2,16512]{2,1,0:T(2,128)(2,1)}), bf16[32,2,16512]{2,1,0:T(2,128)(2,1)}) %all-gather.5.cloned.1.call-update) | async-done | bytes 2113552 | tf_op jit(solution)/shard_map/all_gather | solution.py:47
  107.2 0.7 convert_bitcast_fusion.1
  108.0 4.1 fusion.60
  112.1 2.6 reshape.152
  114.7 1.6 reshape.151
  116.3 4.1 fusion.20
  120.4 0.8 copy.43
  121.2 5.4 %all-to-all-start.1 = ((f32[2,64,256]{2,0,1:T(2,128)}), f32[2,64,256]{2,0,1:T(2,128)S(1)}, u32[]{:S(2)}, u32[]{:S(2)}) async-start(f32[2,64,256]{2,0,1:T(2,128)} %copy.43), calls=%async_computation.1 | async-start | bytes 262144 | tf_op jit(solution)/shard_map/all_to_all | solution.py:70
  126.7 2.5 reshape.119
  129.2 4.8 %all-to-all-done.1 = f32[2,64,256]{2,0,1:T(2,128)S(1)} async-done(((f32[2,64,256]{2,0,1:T(2,128)}), f32[2,64,256]{2,0,1:T(2,128)S(1)}, u32[]{:S(2)}, u32[]{:S(2)}) %all-to-all-start.1) | async-done | bytes 131104 | tf_op jit(solution)/shard_map/all_to_all | solution.py:70
  134.7 96.2 %all-reduce.1 = (f32[32,32]{0,1:T(8,128)S(1)}, f32[32,32]{0,1:T(8,128)S(1)}) all-reduce(f32[32,32]{0,1:T(8,128)S(1)} %convolution_bitcast_fusion.3, f32[32,32]{0,1:T(8,128)S(1)} %convolution_bitcast_fusion.2), channel_id=1, replica_groups=mesh['member'=16,'dp'=32] {'member','dp'}, use_global_device_ids=true, to_apply=%region_1.0 | all-reduce | flops 2048 | bytes 16384 | tf_op jit(solution)/shard_map/psum | solution.py:82
  231.0 2.9 cholesky.44
  235.2 2.4 custom-call.11
  238.0 4.2 convolution_add_fusion
  243.0 80.7 %all-gather.7.cloned.1.call-done = bf16[32,2,16512]{2,1,0:T(2,128)(2,1)} async-done(((bf16[1,2,16512]{2,1,0:T(2,128)(2,1)}), bf16[32,2,16512]{2,1,0:T(2,128)(2,1)}) %all-gather.7.cloned.1.call-update) | async-done | bytes 2113552 | tf_op jit(solution)/shard_map/all_gather | solution.py:47
  323.7 4.0 fusion.59
  327.7 2.6 reshape.122
  330.4 0.7 convert_bitcast_fusion
  331.1 1.6 reshape.153
  332.8 3.2 fusion.1
  336.0 0.8 fusion.17
  337.0 13.8 %all_to_all.35 = f32[2,64,256]{2,0,1:T(2,128)S(1)} all-to-all(f32[2,64,256]{2,0,1:T(2,128)S(1)} %copy.55), channel_id=1, replica_groups=mesh['member'=16,'dp'=32] {'member'}, dimensions={1} | all-to-all | bytes 262144 | tf_op jit(solution)/shard_map/all_to_all | solution.py:70
  351.4 96.0 %all-reduce = (f32[32,32]{0,1:T(8,128)S(1)}, f32[32,32]{0,1:T(8,128)S(1)}) all-reduce(f32[32,32]{0,1:T(8,128)S(1)} %convolution_bitcast_fusion.1, f32[32,32]{0,1:T(8,128)S(1)} %convolution_bitcast_fusion), channel_id=1, replica_groups=mesh['member'=16,'dp'=32] {'member','dp'}, use_global_device_ids=true, to_apply=%region_6.10 | all-reduce | flops 2048 | bytes 16384 | tf_op jit(solution)/shard_map/psum | solution.py:82
  447.5 2.9 cholesky.55
  451.7 2.4 custom-call.13
  454.6 1.1 convolution_add_fusion.1
  (56 shorter events, 9.8 us)
Async XLA Ops:
  7.2 109.1 %copy-start = (bf16[256,64]{0,1:T(8,128)(2,1)S(1)}, bf16[256,64]{0,1:T(8,128)(2,1)}, u32[]{:S(2)}) copy-start(bf16[256,64]{0,1:T(8,128)(2,1)} %param.12) | copy-start | bytes 98308
  7.2 100.1 %all-gather.5.cloned.1.call-start = ((), (), s32[]{:S(2)}) async-start(), calls=%async_computation.3 | async-start | bytes 2179584 | tf_op jit(solution)/shard_map/all_gather | solution.py:47
  14.0 107.2 %all-to-all-start = ((f32[16,2,16576]{2,1,0:T(2,128)}), f32[16,2,16576]{2,1,0:T(2,128)S(1)}, u32[]{:S(2)}, u32[]{:S(2)}) async-start(f32[16,2,16576]{2,1,0:T(2,128)} %stack.2), calls=%async_computation | async-start | bytes 4259840 | tf_op jit(solution)/shard_map/all_to_all | solution.py:9
  112.0 4.2 copy-start.4
  116.3 10.3 %copy-start.2 = (bf16[2,32,4,256]{3,2,1,0:T(4,128)(2,1)S(1)}, bf16[2,32,4,256]{3,2,1,0:T(4,128)(2,1)}, u32[]{:S(2)}) copy-start(bf16[2,32,4,256]{3,2,1,0:T(4,128)(2,1)} %param.14) | copy-start | bytes 393220
  121.2 12.8 %all-to-all-start.1 = ((f32[2,64,256]{2,0,1:T(2,128)}), f32[2,64,256]{2,0,1:T(2,128)S(1)}, u32[]{:S(2)}, u32[]{:S(2)}) async-start(f32[2,64,256]{2,0,1:T(2,128)} %copy.43), calls=%async_computation.1 | async-start | bytes 262144 | tf_op jit(solution)/shard_map/all_to_all | solution.py:70
  126.6 197.1 %all-gather.7.cloned.1.call-start = ((), (), s32[]{:S(2)}) async-start(), calls=%async_computation.4 | async-start | bytes 2179584 | tf_op jit(solution)/shard_map/all_gather | solution.py:47
  126.7 7.4 %copy-start.3 = (f32[4,256]{1,0:T(4,128)S(1)}, f32[4,256]{1,0:T(4,128)}, u32[]{:S(2)}) copy-start(f32[4,256]{1,0:T(4,128)} %param.13) | copy-start | bytes 12292
  332.8 3.2 copy-start.1
Sparse Core Ops, SparseCore 0:
  11.4 95.8 all-gather.4
  243.0 80.6 all-gather.6
